TPU v7x, 32 devices: a whole 2x2x4 slice. The times are simulated.
32 devices in a mesh: ctx: 8 (over y, x, core), head: 4 (over z).
Axes of the slice: x: 2, y: 2, z: 4, core: 2. Of those that a mesh axis runs over, the one named last changes fastest.
Arguments:
- query_rows: bfloat16 [6144, 4096], P('ctx', 'head'), may hold values from -6 to 6
- key_rows: bfloat16 [6144, 4096], P('ctx', 'head'), may hold values from -3.5 to 3.5
- value_rows: bfloat16 [6144, 4096], P('ctx', 'head'), may hold values from -6 to 6
- cluster_ids: int32 [32, 6144, 1], P('head', 'ctx'), may hold values from 0 to 255; in each aligned block of 768 rows (0 to 767, 768 to 1535, ..., all dimensions but the last counted through in order) at most 6 rows name the same one
- centroids: float32 [32, 256, 128], P('head', 'ctx'), may hold values from -6 to 6
- out_weight: bfloat16 [4096, 4096], P(None, 'head'), may hold values from -0.09375 to 0.09375
Outputs:
- layer_output: bfloat16 [6144, 4096], P('ctx', 'head')
- new_centroids: float32 [32, 256, 128], P('head', 'ctx')
Inputs may be any that keep to these rules, and one draw needn't show every extreme that they name: `cluster_ids`: in each aligned block of 768 tokens of one head (the tokens of one index of ctx), no cluster is named by more than 6 tokens, a bound that some block reaches.
All inputs are finite; a program needn't handle non-finite values.
Results may differ from a plain program's by a relative error of at most 0.014.
Values may be sent and summed in bfloat16 or wider, within the bound.
No kernel may reach another device: no remote copies, remote signals or barrier semaphores. Data moves between devices by JAX's collectives and lax.ppermute only.
A program may use at most 128 MiB of HBM per device.

v0:
```python
import jax
import jax.numpy as jnp
from jax import lax
from jax.sharding import PartitionSpec as P

CLUSTERS = 256
prior_weight = 64.0


def slot_targets(labels, per_owner, slot_count):
    length = labels.shape[1]
    order_ids = jnp.arange(length, dtype=jnp.int32)
    same_label = labels[:, :, None] == labels[:, None, :]
    earlier = order_ids[None, :] < order_ids[:, None]
    token_rank = jnp.sum((same_label & earlier[None]).astype(jnp.int32), axis=2)
    owner_of = labels // per_owner
    local_of = labels % per_owner
    return owner_of * (slot_count * per_owner) + token_rank * per_owner + local_of


def attend_blocks(recv, counts_recv, per_owner, head_dim):
    heads_here, sources, width_slots, _ = recv.shape
    slot_count = width_slots // per_owner
    row_count = sources * slot_count
    view = recv.reshape(heads_here, row_count, per_owner, 3 * head_dim)
    query_view = view[..., :head_dim]
    key_view = view[..., head_dim : 2 * head_dim]
    value_view = view[..., 2 * head_dim :]
    rank_ids = jnp.arange(slot_count, dtype=jnp.int32)
    valid = rank_ids[None, None, :, None] < counts_recv[:, :, None, :]
    valid = jnp.transpose(valid.reshape(heads_here, row_count, per_owner), (0, 2, 1))
    row_ids = jnp.arange(row_count, dtype=jnp.int32)
    causal = row_ids[None, :] <= row_ids[:, None]
    allowed = valid[:, :, None, :] & causal[None, None]
    scores = jnp.einsum(
        "hicd,hjcd->hcij", query_view, key_view, preferred_element_type=jnp.float32
    ) * head_dim ** (-0.5)
    scores = jnp.where(allowed, scores, jnp.float32(-1e30))
    top_score = jnp.max(scores, axis=3, keepdims=True)
    weights = jnp.exp(scores - top_score)
    totals = jnp.sum(weights, axis=3, keepdims=True)
    attention_weights = (weights / totals).astype(jnp.bfloat16)
    result = jnp.einsum(
        "hcij,hjcd->hicd", attention_weights, value_view, preferred_element_type=jnp.float32
    ).astype(jnp.bfloat16)
    key_sums = jnp.sum(key_view.astype(jnp.float32), axis=1)
    key_counts = jnp.sum(counts_recv, axis=1).astype(jnp.float32)
    return (result.reshape(heads_here, sources, width_slots, head_dim), key_sums, key_counts)


def local(query_rows, key_rows, value_rows, cluster_ids, centroids, out_weight):
    ctx_count = lax.axis_size("ctx")
    token_count = query_rows.shape[0]
    heads_here = cluster_ids.shape[0]
    head_dim = query_rows.shape[1] // heads_here
    clusters = CLUSTERS
    per_owner = clusters // ctx_count
    slot_count = 2 * token_count // clusters
    row_total = clusters * slot_count
    labels = cluster_ids[:, :, 0]
    targets = slot_targets(labels, per_owner, slot_count)
    head_ids = jnp.arange(heads_here, dtype=jnp.int32)
    token_ids = jnp.arange(token_count, dtype=jnp.int32)
    token_at = jnp.full((heads_here, row_total), token_count, jnp.int32)
    token_at = token_at.at[head_ids[:, None], targets].set(
        jnp.broadcast_to(token_ids[None, :], targets.shape), unique_indices=True
    )
    filled_slot = token_at < token_count
    flat_index = jnp.where(filled_slot, token_at * heads_here + head_ids[:, None], 0)

    def pick(rows):
        table = rows.reshape(token_count * heads_here, head_dim)
        got = jnp.take(table, flat_index, axis=0)
        return jnp.where(filled_slot[..., None], got, jnp.zeros_like(got))

    send = jnp.concatenate((pick(query_rows), pick(key_rows), pick(value_rows)), axis=2).reshape(
        heads_here, ctx_count, slot_count * per_owner, 3 * head_dim
    )
    one_hot = labels[:, :, None] == jnp.arange(clusters, dtype=jnp.int32)[None, None, :]
    counts_send = jnp.sum(one_hot.astype(jnp.int32), axis=1).reshape(
        heads_here, ctx_count, per_owner
    )
    recv = lax.all_to_all(send, "ctx", split_axis=1, concat_axis=1, tiled=True)
    counts_recv = lax.all_to_all(counts_send, "ctx", split_axis=1, concat_axis=1, tiled=True)
    result, key_sums, key_counts = attend_blocks(recv, counts_recv, per_owner, head_dim)
    new_centroids = (prior_weight * centroids + key_sums) / (prior_weight + key_counts[:, :, None])
    returned = lax.all_to_all(result, "ctx", split_axis=1, concat_axis=1, tiled=True)
    returned_flat = returned.reshape(heads_here * row_total, head_dim)
    back_index = jnp.transpose(targets + head_ids[:, None] * row_total, (1, 0))
    attended = jnp.take(returned_flat, back_index, axis=0).reshape(
        token_count, heads_here * head_dim
    )
    mixed_total = jnp.dot(
        lax.all_gather(attended, "head", axis=1, tiled=True),
        out_weight,
        preferred_element_type=jnp.float32,
    )
    return (mixed_total.astype(jnp.bfloat16), new_centroids)


def solution(mesh):
    placed = (
        P("ctx", "head"),
        P("ctx", "head"),
        P("ctx", "head"),
        P("head", "ctx", None),
        P("head", "ctx", None),
        P(None, "head"),
    )
    return jax.shard_map(
        local,
        mesh=mesh,
        in_specs=placed,
        out_specs=(P("ctx", "head"), P("head", "ctx", None)),
        check_vma=False,
    )
```

profile of v0, /device:TPU:0, one launch (start us, length us, event | category | flops | bytes accessed | tf_op | source)
XLA Modules:
  0.0 540.2 jit_solution(5230525954035740918)
XLA Ops:
  7.9 1.2 convert_reduce_fusion.2
  9.8 5.2 all-to-all-start.1
  15.2 4.4 convert_reduce_fusion
  19.6 0.8 compare_select_fusion.1
  21.9 23.0 %scatter_custom_fusion = s32[12288]{0:T(1024)S(1)} fusion(s32[6144]{0:T(1024)S(1)} %reshape.145, s32[6144]{0:T(1024)S(1)} %reshape.147, s32[]{:T(128)} %constant.74.clone.1), kind=kCustom, calls=%fused_computation.63 | custom fusion | bytes 49156
  45.1 2.6 reshape.97
  47.6 2.6 reshape.98
  50.2 43.3 %gather_fusion.1 = bf16[12288,128]{1,0:T(8,128)(2,1)} fusion(bf16[6144,128]{1,0:T(8,128)(2,1)S(1)} %reshape.97, s32[12288]{0:T(1024)S(1)} %broadcast_clamp_fusion), kind=kCustom, calls=%fused_computation.clone | custom fusion | bytes 6340608 | tf_op jit(solution)/shard_map/jit(_take)/gather | solution.py:73
  93.5 43.3 %gather_fusion.2 = bf16[12288,128]{1,0:T(8,128)(2,1)} fusion(bf16[6144,128]{1,0:T(8,128)(2,1)S(1)} %reshape.98, s32[12288]{0:T(1024)S(1)} %broadcast_clamp_fusion), kind=kCustom, calls=%fused_computation.1.clone | custom fusion | bytes 6340608 | tf_op jit(solution)/shard_map/jit(_take)/gather | solution.py:73
  137.5 43.3 %gather_fusion.3 = bf16[12288,128]{1,0:T(8,128)(2,1)} fusion(bf16[6144,128]{1,0:T(8,128)(2,1)S(1)} %reshape.99, s32[12288]{0:T(1024)S(1)} %broadcast_clamp_fusion), kind=kCustom, calls=%fused_computation.2.clone | custom fusion | bytes 6340608 | tf_op jit(solution)/shard_map/jit(_take)/gather | solution.py:73
  180.8 6.5 %select_select_fusion.2 = (bf16[8,1536,128]{2,1,0:T(8,128)(2,1)S(1)}, bf16[8,1536,128]{2,1,0:T(8,128)(2,1)S(1)}, bf16[8,1536,128]{2,1,0:T(8,128)(2,1)S(1)}) fusion(bf16[8,1536,128]{2,1,0:T(8,128)(2,1)} %bitcast.43, pred[8,1536]{1,0:T(8,128)(4,1)S(1)} %get-tuple-element.5, pred[8,1536]{1,0:T(8,128)(4,1)S(1)} %reshape.110, bf16[8,1536,128]{2,1,0:T(8,128)(2,1)} %bitcast.44, ...), kind=kLoop, calls=%fused_computation.21 | loop fusion | flops 9437184 | bytes 18898944 | tf_op jit(solution)/shard_map/jit(_where)/select_n | solution.py:74
  187.3 4.7 pad_maximum_fusion
  191.9 8.6 %copy.49 = bf16[8,8,192,384]{3,2,0,1:T(8,128)(2,1)} copy(bf16[8,8,192,384]{3,2,1,0:T(8,128)(2,1)} %bitcast.41) | data formatting | bytes 18874368 | tf_op jit(solution)/shard_map/reshape | solution.py:76
  200.5 5.2 all-to-all-start
  207.4 103.8 %all-to-all-done = bf16[8,8,192,384]{3,2,0,1:T(8,128)(2,1)} async-done(((bf16[8,8,192,384]{3,2,0,1:T(8,128)(2,1)}), bf16[8,8,192,384]{3,2,0,1:T(8,128)(2,1)}, u32[]{:S(2)}, u32[]{:S(2)}) %all-to-all-start) | async-done | bytes 9437216 | tf_op jit(solution)/shard_map/all_to_all | solution.py:83
  311.2 8.6 %copy.50 = bf16[8,8,192,384]{3,2,1,0:T(8,128)(2,1)} copy(bf16[8,8,192,384]{3,2,0,1:T(8,128)(2,1)} %all-to-all-done) | data formatting | bytes 18874368 | tf_op jit(solution)/shard_map/all_to_all | solution.py:83
  319.8 4.6 fusion.34
  324.4 2.1 fusion.3
  326.5 3.5 fusion.35
  330.0 2.2 convert_bitcast_fusion
  332.2 0.8 copy.57
  333.0 2.0 copy.58
  335.0 4.6 all-to-all-start.2
  340.6 36.9 %all-to-all-done.2 = bf16[8,8,192,128]{3,2,0,1:T(8,128)(2,1)} async-done(((bf16[8,8,192,128]{3,2,0,1:T(8,128)(2,1)}), bf16[8,8,192,128]{3,2,0,1:T(8,128)(2,1)}, u32[]{:S(2)}, u32[]{:S(2)}) %all-to-all-start.2) | async-done | bytes 3145760 | tf_op jit(solution)/shard_map/all_to_all | solution.py:87
  377.4 2.2 copy.59
  379.6 22.3 %gather_fusion = bf16[6144,128]{1,0:T(8,128)(2,1)} fusion(bf16[12288,128]{1,0:T(8,128)(2,1)S(1)} %bitcast.39, s32[6144]{0:T(1024)S(1)} %broadcast_clamp_fusion.1), kind=kCustom, calls=%fused_computation.3 | custom fusion | bytes 3170304 | tf_op jit(solution)/shard_map/jit(_take)/gather | solution.py:90
  401.9 2.9 bitcast_select_fusion
  404.7 1.6 copy.83
  406.4 0.8 copy-done.1
  407.2 1.8 convert_reduce_fusion.1
  409.7 111.5 %all-gather.2.cloned.1.call-done = bf16[768,4096]{1,0:T(8,128)(2,1)} async-done(((bf16[768,1024]{1,0:T(8,128)(2,1)}), bf16[768,4096]{1,0:T(8,128)(2,1)}) %all-gather.2.cloned.1.call-update) | async-done | bytes 6291472 | tf_op jit(solution)/shard_map/all_gather | solution.py:94
  521.3 12.1 %convolution_convert_fusion = bf16[768,1024]{1,0:T(8,128)(2,1)} fusion(bf16[768,4096]{1,0:T(8,128)(2,1)} %all-gather.2.cloned.1.call-done, bf16[4096,1024]{1,0:T(8,128)(2,1)} %param.13), kind=kOutput, calls=%fused_computation.30 | convolution fusion | flops 6443237376 | bytes 16252928 | tf_op jit(solution)/shard_map/dot_general | solution.py:93
  (49 shorter events, 7.4 us)
Async XLA Ops:
  9.8 190.7 %all-to-all-start.1 = ((s32[8,1,256]{2,1,0:T(1,128)}), s32[8,1,256]{2,1,0:T(1,128)S(1)}, u32[]{:S(2)}, u32[]{:S(2)}) async-start(s32[8,1,256]{2,1,0:T(1,128)} %reshape.173), calls=%async_computation.1 | async-start | bytes 16384 | tf_op jit(solution)/shard_map/all_to_all | solution.py:84
  93.5 43.3 %copy-start.2 = (bf16[768,1024]{1,0:T(8,128)(2,1)S(1)}, bf16[768,1024]{1,0:T(8,128)(2,1)}, u32[]{:S(2)}) copy-start(bf16[768,1024]{1,0:T(8,128)(2,1)} %param.10) | copy-start | bytes 4718596
  200.5 110.6 %all-to-all-start = ((bf16[8,8,192,384]{3,2,0,1:T(8,128)(2,1)}), bf16[8,8,192,384]{3,2,0,1:T(8,128)(2,1)}, u32[]{:S(2)}, u32[]{:S(2)}) async-start(bf16[8,8,192,384]{3,2,0,1:T(8,128)(2,1)} %copy.49), calls=%async_computation | async-start | bytes 18874368 | tf_op jit(solution)/shard_map/all_to_all | solution.py:83
  324.4 2.2 copy-start
  335.0 4.9 copy-start.3
  335.0 42.5 %all-to-all-start.2 = ((bf16[8,8,192,128]{3,2,0,1:T(8,128)(2,1)}), bf16[8,8,192,128]{3,2,0,1:T(8,128)(2,1)}, u32[]{:S(2)}, u32[]{:S(2)}) async-start(bf16[8,8,192,128]{3,2,0,1:T(8,128)(2,1)} %copy.58), calls=%async_computation.2 | async-start | bytes 6291456 | tf_op jit(solution)/shard_map/all_to_all | solution.py:87
  339.5 181.7 %all-gather.2.cloned.1.call-start = ((), (), s32[]{:S(2)}) async-start(), calls=%async_computation.3 | async-start | bytes 7864320 | tf_op jit(solution)/shard_map/all_gather | solution.py:94
  404.7 2.5 copy-start.1
  406.3 2.6 copy-start.4
Sparse Core Ops, SparseCore 0:
  406.5 114.7 all-gather.1
where the time goes:
time: 541 us; the launch traced here: 540 us
  waiting for transfers between devices  252 us (47%)
  local copies, waits for them, and re-layouts  213 us (39%)
  other arithmetic  28.9 us (5%)
  matrix products  16.4 us (3%)
  starting transfers between devices  15.2 us (3%)
  between operations  14.4 us (3%)
    gather x3, local copies, waits for them, and re-layouts, pick(): got = jnp.take(table, flat_index, axis=0)  130 us
    all_gather x1, waiting for transfers between devices, local(): lax.all_gather(attended, 'head', axis=1, tiled=True)  112 us
    all_to_all x1, waiting for transfers between devices, local(): recv = lax.all_to_all(send, 'ctx', split_axis=1, concat_axis=1, tiled=True)  104 us
    all_to_all x1, waiting for transfers between devices, local(): lax.all_to_all(result, 'ctx', split_axis=1, concat_axis=1, tiled=True)  36.9 us
    unnamed x16, local copies, waits for them, and re-layouts  26.9 us
    gather x1, local copies, waits for them, and re-layouts, local(): jnp.take(returned_flat, back_index, axis=0)  22.3 us
    dot_general x1, matrix products, local(): jnp.dot(lax.all_gather(attended, 'head', axis=1, tiled=True), out_weight,...  12.1 us
  transfers between devices with their start and end apart: 4, of which 3 were waited for; matrix products, arithmetic and copies ran while one was open for 35% of the time, Pallas kernels for 0%

commit v1 on v0

--- a/solution.py
+++ b/solution.py
@@ -5,6 +5,27 @@
 
 CLUSTERS = 256
 prior_weight = 64.0
+
+
+def gather_around(array, axis, dim):
+    devices, position, rows = (lax.axis_size(axis), lax.axis_index(axis), array.shape[dim])
+    ahead = [(i, (i + 1) % devices) for i in range(devices)]
+    downward = [(i, (i - 1) % devices) for i in range(devices)]
+    whole = jnp.zeros((*array.shape[:dim], devices * rows, *array.shape[dim + 1 :]), array.dtype)
+    whole = lax.dynamic_update_slice_in_dim(whole, array, position * rows, axis=dim)
+    from_left = from_right = array
+    half = devices // 2
+    for turn in range(1, half + 1):
+        from_left = lax.ppermute(from_left, axis, ahead)
+        whole = lax.dynamic_update_slice_in_dim(
+            whole, from_left, (position - turn) % devices * rows, axis=dim
+        )
+        if turn < devices - half:
+            from_right = lax.ppermute(from_right, axis, downward)
+            whole = lax.dynamic_update_slice_in_dim(
+                whole, from_right, (position + turn) % devices * rows, axis=dim
+            )
+    return whole
 
 
 def slot_targets(labels, per_owner, slot_count):
@@ -91,9 +112,7 @@
         token_count, heads_here * head_dim
     )
     mixed_total = jnp.dot(
-        lax.all_gather(attended, "head", axis=1, tiled=True),
-        out_weight,
-        preferred_element_type=jnp.float32,
+        gather_around(attended, "head", 1), out_weight, preferred_element_type=jnp.float32
     )
     return (mixed_total.astype(jnp.bfloat16), new_centroids)
 

time: 541 us -> 515 us (0.952)
  waiting for transfers between devices: 252 us -> 203 us
  starting transfers between devices: 15.2 us -> 48 us
  between operations: 14.4 us -> 1.06 us
  local copies, waits for them, and re-layouts: 213 us -> 220 us
    all_gather x1 -> x0, waiting for transfers between devices: 112 us -> none  [local(): lax.all_gather(attended, 'head', axis=1, tiled=True)]
    ppermute x0 -> x3, waiting for transfers between devices: none -> 62.1 us  [the longest x2 62.1 us: gather_around(): from_left = lax.ppermute(from_left, axis, ahead)]
    ppermute x0 -> x3, starting transfers between devices: none -> 32.8 us  [the longest x2 30.6 us: gather_around(): from_left = lax.ppermute(from_left, axis, ahead)]
    unnamed x16 -> x24, local copies, waits for them, and re-layouts: 26.9 us -> 27.9 us
  transfers between devices with their start and end apart: 4 -> 6, of which waited for: 3 -> 4; matrix products, arithmetic and copies ran while one was open for 35% -> 38% of each run, Pallas kernels for 0% -> 0%
where the time goes in v1:
time: 515 us; the launch traced here: 513 us
  local copies, waits for them, and re-layouts  220 us (43%)
  waiting for transfers between devices  203 us (39%)
  starting transfers between devices  48 us (9%)
  other arithmetic  29 us (6%)
  matrix products  12.1 us (2%)
    gather x3, local copies, waits for them, and re-layouts, pick(): got = jnp.take(table, flat_index, axis=0)  130 us
    all_to_all x1, waiting for transfers between devices, local(): recv = lax.all_to_all(send, 'ctx', split_axis=1, concat_axis=1, tiled=True)  104 us
    ppermute x2, waiting for transfers between devices, gather_around(): from_left = lax.ppermute(from_left, axis, ahead)  62.1 us
    all_to_all x1, waiting for transfers between devices, local(): lax.all_to_all(result, 'ctx', split_axis=1, concat_axis=1, tiled=True)  36.9 us
    ppermute x2, starting transfers between devices, gather_around(): from_left = lax.ppermute(from_left, axis, ahead)  30.6 us
    unnamed x24, local copies, waits for them, and re-layouts  27.9 us
    gather x1, local copies, waits for them, and re-layouts, local(): jnp.take(returned_flat, back_index, axis=0)  22.3 us
  transfers between devices with their start and end apart: 6, of which 4 were waited for; matrix products, arithmetic and copies ran while one was open for 38% of the time, Pallas kernels for 0%

profile of v1, /device:TPU:0, one launch (start us, length us, event | category | flops | bytes accessed | tf_op | source)
XLA Modules:
  0.0 513.2 jit_solution(12742501409984481964)
XLA Ops:
  3.3 5.2 %all-to-all-start.1 = ((s32[8,1,256]{2,1,0:T(1,128)}), s32[8,1,256]{2,1,0:T(1,128)S(1)}, u32[]{:S(2)}, u32[]{:S(2)}) async-start(s32[8,1,256]{2,1,0:T(1,128)} %reshape.173), calls=%async_computation.1 | async-start | bytes 16384 | tf_op jit(solution)/shard_map/all_to_all | solution.py:105
  8.7 4.4 convert_reduce_fusion
  15.3 23.0 %scatter_custom_fusion = s32[12288]{0:T(1024)S(1)} fusion(s32[6144]{0:T(1024)S(1)} %reshape.145, s32[6144]{0:T(1024)S(1)} %reshape.147, s32[]{:T(128)} %constant.103.clone.1), kind=kCustom, calls=%fused_computation.63 | custom fusion | bytes 49156
  38.5 2.6 reshape.97
  41.1 2.6 reshape.98
  43.6 43.3 %gather_fusion.1 = bf16[12288,128]{1,0:T(8,128)(2,1)} fusion(bf16[6144,128]{1,0:T(8,128)(2,1)S(1)} %reshape.97, s32[12288]{0:T(1024)S(1)} %broadcast_clamp_fusion), kind=kCustom, calls=%fused_computation.clone | custom fusion | bytes 6340608 | tf_op jit(solution)/shard_map/jit(_take)/gather | solution.py:94
  87.0 43.3 %gather_fusion.2 = bf16[12288,128]{1,0:T(8,128)(2,1)} fusion(bf16[6144,128]{1,0:T(8,128)(2,1)S(1)} %reshape.98, s32[12288]{0:T(1024)S(1)} %broadcast_clamp_fusion), kind=kCustom, calls=%fused_computation.1.clone | custom fusion | bytes 6340608 | tf_op jit(solution)/shard_map/jit(_take)/gather | solution.py:94
  131.0 43.3 %gather_fusion.3 = bf16[12288,128]{1,0:T(8,128)(2,1)} fusion(bf16[6144,128]{1,0:T(8,128)(2,1)S(1)} %reshape.99, s32[12288]{0:T(1024)S(1)} %broadcast_clamp_fusion), kind=kCustom, calls=%fused_computation.2.clone | custom fusion | bytes 6340608 | tf_op jit(solution)/shard_map/jit(_take)/gather | solution.py:94
  174.3 6.5 %select_select_fusion.2 = (bf16[8,1536,128]{2,1,0:T(8,128)(2,1)S(1)}, bf16[8,1536,128]{2,1,0:T(8,128)(2,1)S(1)}, bf16[8,1536,128]{2,1,0:T(8,128)(2,1)S(1)}) fusion(bf16[8,1536,128]{2,1,0:T(8,128)(2,1)} %bitcast.47, pred[8,1536]{1,0:T(8,128)(4,1)S(1)} %get-tuple-element.5, pred[8,1536]{1,0:T(8,128)(4,1)S(1)} %reshape.110, bf16[8,1536,128]{2,1,0:T(8,128)(2,1)} %bitcast.48, ...), kind=kLoop, calls=%fused_computation.21 | loop fusion | flops 9437184 | bytes 18898944 | tf_op jit(solution)/shard_map/jit(_where)/select_n | solution.py:95
  180.7 4.7 pad_maximum_fusion
  185.4 8.6 %copy.49 = bf16[8,8,192,384]{3,2,0,1:T(8,128)(2,1)} copy(bf16[8,8,192,384]{3,2,1,0:T(8,128)(2,1)} %bitcast.43) | data formatting | bytes 18874368 | tf_op jit(solution)/shard_map/reshape | solution.py:97
  194.0 5.2 %all-to-all-start = ((bf16[8,8,192,384]{3,2,0,1:T(8,128)(2,1)}), bf16[8,8,192,384]{3,2,0,1:T(8,128)(2,1)}, u32[]{:S(2)}, u32[]{:S(2)}) async-start(bf16[8,8,192,384]{3,2,0,1:T(8,128)(2,1)} %copy.49), calls=%async_computation | async-start | bytes 18874368 | tf_op jit(solution)/shard_map/all_to_all | solution.py:104
  200.9 103.8 %all-to-all-done = bf16[8,8,192,384]{3,2,0,1:T(8,128)(2,1)} async-done(((bf16[8,8,192,384]{3,2,0,1:T(8,128)(2,1)}), bf16[8,8,192,384]{3,2,0,1:T(8,128)(2,1)}, u32[]{:S(2)}, u32[]{:S(2)}) %all-to-all-start) | async-done | bytes 9437216 | tf_op jit(solution)/shard_map/all_to_all | solution.py:104
  304.6 8.6 %copy.50 = bf16[8,8,192,384]{3,2,1,0:T(8,128)(2,1)} copy(bf16[8,8,192,384]{3,2,0,1:T(8,128)(2,1)} %all-to-all-done) | data formatting | bytes 18874368 | tf_op jit(solution)/shard_map/all_to_all | solution.py:104
  313.2 4.6 fusion.34
  317.8 2.1 fusion.3
  320.0 3.5 fusion.35
  323.5 2.2 convert_bitcast_fusion
  326.5 2.0 copy.58
  328.4 4.8 all-to-all-start.2
  334.0 36.9 %all-to-all-done.2 = bf16[8,8,192,128]{3,2,0,1:T(8,128)(2,1)} async-done(((bf16[8,8,192,128]{3,2,0,1:T(8,128)(2,1)}), bf16[8,8,192,128]{3,2,0,1:T(8,128)(2,1)}, u32[]{:S(2)}, u32[]{:S(2)}) %all-to-all-start.2) | async-done | bytes 3145760 | tf_op jit(solution)/shard_map/all_to_all | solution.py:108
  370.9 2.2 copy.59
  373.1 22.3 %gather_fusion = bf16[6144,128]{1,0:T(8,128)(2,1)} fusion(bf16[12288,128]{1,0:T(8,128)(2,1)S(1)} %bitcast.41, s32[6144]{0:T(1024)S(1)} %broadcast_clamp_fusion.1), kind=kCustom, calls=%fused_computation.3 | custom fusion | bytes 3170304 | tf_op jit(solution)/shard_map/jit(_take)/gather | solution.py:111
  395.3 3.0 bitcast_select_fusion
  399.5 1.6 copy.85
  402.7 2.2 collective-permute-start.1
  405.0 35.6 %collective-permute-done = bf16[768,1024]{1,0:T(8,128)(2,1)} collective-permute-done((bf16[768,1024]{1,0:T(8,128)(2,1)}, bf16[768,1024]{1,0:T(8,128)(2,1)}, u32[]{:S(2)}, u32[]{:S(2)}) %collective-permute-start) | collective-permute-done | bytes 1572896 | tf_op jit(solution)/shard_map/ppermute | solution.py:19
  440.6 29.0 %collective-permute-start.2 = (bf16[768,1024]{1,0:T(8,128)(2,1)}, bf16[768,1024]{1,0:T(8,128)(2,1)}, u32[]{:S(2)}, u32[]{:S(2)}) collective-permute-start(bf16[768,1024]{1,0:T(8,128)(2,1)} %collective-permute-done), channel_id=1, source_target_pairs={{0,1},{1,2},{2,3},{3,0},{4,5},{5,6},{6,7},{7,4},{8,9},{9,10},{10,1... | collective-permute-start | bytes 4718600 | tf_op jit(solution)/shard_map/ppermute | solution.py:19
  469.6 1.8 convert_reduce_fusion.1
  473.9 1.8 constant_dynamic-update-slice_fusion.2
  477.3 26.4 %collective-permute-done.2 = bf16[768,1024]{1,0:T(8,128)(2,1)} collective-permute-done((bf16[768,1024]{1,0:T(8,128)(2,1)}, bf16[768,1024]{1,0:T(8,128)(2,1)}, u32[]{:S(2)}, u32[]{:S(2)}) %collective-permute-start.2) | collective-permute-done | bytes 1572896 | tf_op jit(solution)/shard_map/ppermute | solution.py:19
  505.4 7.8 %convolution_convert_fusion = bf16[768,1024]{1,0:T(8,128)(2,1)} fusion(bf16[768,4096]{1,0:T(8,128)(2,1)S(1)} %constant_dynamic-update-slice_fusion, bf16[4096,1024]{1,0:T(8,128)(2,1)S(1)} %bitcast.56), kind=kOutput, calls=%fused_computation.30 | convolution fusion | flops 6443237376 | bytes 16252928 | tf_op jit(solution)/shard_map/dot_general | solution.py:114
  (66 shorter events, 17.6 us)
Async XLA Ops:
  3.3 190.7 %all-to-all-start.1 = ((s32[8,1,256]{2,1,0:T(1,128)}), s32[8,1,256]{2,1,0:T(1,128)S(1)}, u32[]{:S(2)}, u32[]{:S(2)}) async-start(s32[8,1,256]{2,1,0:T(1,128)} %reshape.173), calls=%async_computation.1 | async-start | bytes 16384 | tf_op jit(solution)/shard_map/all_to_all | solution.py:105
  87.0 43.3 %copy-start.4 = (bf16[768,1024]{1,0:T(8,128)(2,1)S(1)}, bf16[768,1024]{1,0:T(8,128)(2,1)}, u32[]{:S(2)}) copy-start(bf16[768,1024]{1,0:T(8,128)(2,1)} %param.10) | copy-start | bytes 4718596
  194.0 110.6 %all-to-all-start = ((bf16[8,8,192,384]{3,2,0,1:T(8,128)(2,1)}), bf16[8,8,192,384]{3,2,0,1:T(8,128)(2,1)}, u32[]{:S(2)}, u32[]{:S(2)}) async-start(bf16[8,8,192,384]{3,2,0,1:T(8,128)(2,1)} %copy.49), calls=%async_computation | async-start | bytes 18874368 | tf_op jit(solution)/shard_map/all_to_all | solution.py:104
  317.8 2.2 copy-start
  328.4 4.8 copy-start.5
  328.4 42.5 %all-to-all-start.2 = ((bf16[8,8,192,128]{3,2,0,1:T(8,128)(2,1)}), bf16[8,8,192,128]{3,2,0,1:T(8,128)(2,1)}, u32[]{:S(2)}, u32[]{:S(2)}) async-start(bf16[8,8,192,128]{3,2,0,1:T(8,128)(2,1)} %copy.58), calls=%async_computation.2 | async-start | bytes 6291456 | tf_op jit(solution)/shard_map/all_to_all | solution.py:108
  395.3 74.3 %copy-start.1 = (bf16[8,48,32,128]{3,2,1,0:T(8,128)(2,1)S(1)}, bf16[8,48,32,128]{3,2,1,0:T(8,128)(2,1)}, u32[]{:S(2)}) copy-start(bf16[8,48,32,128]{3,2,1,0:T(8,128)(2,1)} %copy-done) | copy-start | bytes 9437188
  398.4 1.1 copy-start.2
  399.5 71.9 %copy-start.6 = (f32[8,32,128]{2,1,0:T(8,128)S(1)}, f32[8,32,128]{2,1,0:T(8,128)}, u32[]{:S(2)}) copy-start(f32[8,32,128]{2,1,0:T(8,128)} %param.12) | copy-start | bytes 393220
  401.1 39.4 %collective-permute-start = (bf16[768,1024]{1,0:T(8,128)(2,1)}, bf16[768,1024]{1,0:T(8,128)(2,1)}, u32[]{:S(2)}, u32[]{:S(2)}) collective-permute-start(bf16[768,1024]{1,0:T(8,128)(2,1)} %bitcast.37), channel_id=1, source_target_pairs={{0,1},{1,2},{2,3},{3,0},{4,5},{5,6},{6,7},{7,4},{8,9},{9,10},{10,1... | collective-permute-start | bytes 4718600 | tf_op jit(solution)/shard_map/ppermute | solution.py:19
  402.7 73.0 %collective-permute-start.1 = (bf16[768,1024]{1,0:T(8,128)(2,1)}, bf16[768,1024]{1,0:T(8,128)(2,1)}, u32[]{:S(2)}, u32[]{:S(2)}) collective-permute-start(bf16[768,1024]{1,0:T(8,128)(2,1)} %bitcast.37), channel_id=1, source_target_pairs={{0,3},{1,0},{2,1},{3,2},{4,7},{5,4},{6,5},{7,6},{8,11},{9,8},{10,9... | collective-permute-start | bytes 4718600 | tf_op jit(solution)/shard_map/ppermute | solution.py:24
  440.6 63.2 %collective-permute-start.2 = (bf16[768,1024]{1,0:T(8,128)(2,1)}, bf16[768,1024]{1,0:T(8,128)(2,1)}, u32[]{:S(2)}, u32[]{:S(2)}) collective-permute-start(bf16[768,1024]{1,0:T(8,128)(2,1)} %collective-permute-done), channel_id=1, source_target_pairs={{0,1},{1,2},{2,3},{3,0},{4,5},{5,6},{6,7},{7,4},{8,9},{9,10},{10,1... | collective-permute-start | bytes 4718600 | tf_op jit(solution)/shard_map/ppermute | solution.py:19
  472.1 1.4 copy-start.3
  472.1 33.3 %slice-start = ((s8[8388608]{0:T(1024)(128)(4,1)}), s8[4194304]{0:T(1024)(128)(4,1)S(1)}, s32[]{:S(2)}) async-start(s8[8388608]{0:T(1024)(128)(4,1)} %bitcast.55), calls=%async_computation.3 | async-start | bytes 8388608
  473.9 31.5 %slice-start.1 = ((s8[8388608]{0:T(1024)(128)(4,1)}), s8[4194304]{0:T(1024)(128)(4,1)S(1)}, s32[]{:S(2)}) async-start(s8[8388608]{0:T(1024)(128)(4,1)} %bitcast.55), calls=%async_computation.4 | async-start | bytes 8388608
